TPU v7x, 128 devices: a whole 4x4x4 slice. The times are simulated.
128 devices in a mesh: gx: 8 (over z, core), gy: 16 (over y, x).
Axes of the slice: x: 4, y: 4, z: 4, core: 2. Of those that a mesh axis runs over, the one named last changes fastest.
Arguments:
- hidden_in: bfloat16 [32768, 3584], P(('gx', 'gy')), may hold values from -6 to 6
- lengths: int32 [8, 4], P('gx'), may hold values from 1 to 2048, 4096 in all within a row
- attn_norm: float32 [3584], replicated, may hold values from 0.5 to 1.5
- qkv_weight: bfloat16 [3584, 4608], P('gx', 'gy'), may hold values from -0.09375 to 0.09375
- qkv_bias: float32 [4608], replicated, may hold values from -5 to 5
Outputs:
- attn: bfloat16 [32768, 3584], P(('gx', 'gy'))
- kv_rows: bfloat16 [32768, 1024], P(('gx', 'gy'))
Inputs may be any that keep to these rules, and one draw needn't show every extreme that they name: Each row of lengths sums to 4096; the longest of each row is exactly 2048.
All inputs are finite; a program needn't handle non-finite values.
Results may differ from a plain program's by a relative error of at most 0.0035.
The roundings to bfloat16 on the way count: a program that leaves them out, or rounds other values in their place, can miss the bound.
Values may be sent and summed in bfloat16 or wider, within the bound.
No kernel may reach another device: no remote copies, remote signals or barrier semaphores. Data moves between devices by JAX's collectives and lax.ppermute only.
A program may use at most 128 MiB of HBM per device.

v0:
```python
import math
import jax
import jax.numpy as jnp
from jax import lax
from jax.sharding import PartitionSpec as P

HEADS = 28
KV_HEADS = 4
HEAD_DIM = 128
key_span = 512


def norm_rows(values, gain):
    wide = values.astype(jnp.float32)
    scale = lax.rsqrt(jnp.mean(wide * wide, axis=1, keepdims=True) + 1e-06)
    return (wide * scale * gain[None, :]).astype(jnp.bfloat16)


def segment_of(index, ends):
    return jnp.sum((ends[None, :] <= index[:, None]).astype(jnp.int32), axis=1)


def rotate(block, pos, heads):
    half = HEAD_DIM // 2
    freqs = 1000000.0 ** (-2.0 * jnp.arange(half, dtype=jnp.float32) / HEAD_DIM)
    angle = pos.astype(jnp.float32)[:, None, None] * freqs[None, None, :]
    wide = block.astype(jnp.float32).reshape(block.shape[0], heads, HEAD_DIM)
    first, second = (wide[..., :half], wide[..., half:])
    turned = jnp.concatenate(
        [
            first * jnp.cos(angle) - second * jnp.sin(angle),
            second * jnp.cos(angle) + first * jnp.sin(angle),
        ],
        axis=2,
    )
    return turned.reshape(block.shape[0], heads * HEAD_DIM).astype(jnp.bfloat16)


def project_joined(normed, weight, bias):
    grouped = lax.all_gather(normed, "gy", axis=0, tiled=True)
    summed = jnp.dot(
        grouped,
        lax.all_gather(weight, "gx", axis=0, tiled=True),
        preferred_element_type=jnp.float32,
    )
    width = weight.shape[1]
    bias_block = lax.dynamic_slice_in_dim(bias, lax.axis_index("gy") * width, width, 0)
    block_out = (summed + bias_block[None, :]).astype(jnp.bfloat16)
    return lax.all_to_all(block_out, "gy", split_axis=0, concat_axis=1, tiled=True)


def on_device(hidden_in, lengths, attn_norm, qkv_weight, qkv_bias):
    rows = hidden_in.shape[0]
    first = lax.axis_index("gy") * rows
    row_lengths = lengths[0]
    qdim = HEADS * HEAD_DIM
    kdim = KV_HEADS * HEAD_DIM
    group = HEADS // KV_HEADS
    normed = norm_rows(hidden_in, attn_norm)
    joined = project_joined(normed, qkv_weight, qkv_bias)
    ends = jnp.cumsum(row_lengths)
    tokens_here = first + jnp.arange(rows, dtype=jnp.int32)
    before = ends[None, :] <= tokens_here[:, None]
    seg_here = jnp.sum(before.astype(jnp.int32), axis=1)
    begin = jnp.sum(jnp.where(before, row_lengths[None, :], 0), axis=1)
    pos = tokens_here - begin
    queries = rotate(joined[:, :qdim], pos, HEADS).reshape(rows, KV_HEADS, group, HEAD_DIM)
    keys = rotate(joined[:, qdim : qdim + kdim], pos, KV_HEADS)
    kv_rows = jnp.concatenate([keys, joined[:, qdim + kdim :]], axis=1)
    scale = 1.0 / HEAD_DIM**0.5

    def attend(carry, piece, start):
        running, total, summed = carry
        key_count = piece.shape[0]
        key_index = start + jnp.arange(key_count, dtype=jnp.int32)
        key_seg = segment_of(key_index, ends)
        key_part = piece[:, :kdim].reshape(key_count, KV_HEADS, HEAD_DIM)
        value_part = piece[:, kdim:].reshape(key_count, KV_HEADS, HEAD_DIM)
        scores = (
            jnp.einsum("rgho,ngo->ghrn", queries, key_part, preferred_element_type=jnp.float32)
            * scale
        )
        allowed = (seg_here[:, None] == key_seg[None, :]) & (
            key_index[None, :] <= tokens_here[:, None]
        )
        newest = jnp.maximum(running, jnp.max(jnp.where(allowed, scores, -1e30), axis=3))
        shrink = jnp.exp(running - newest)
        weights = jnp.where(allowed, jnp.exp(scores - newest[..., None]), 0.0)
        total = total * shrink + jnp.sum(weights, axis=3)
        summed = summed * shrink[..., None] + jnp.einsum(
            "ghrn,ngo->ghro",
            weights.astype(jnp.bfloat16),
            value_part,
            preferred_element_type=jnp.float32,
        )
        return (newest, total, summed)

    def visit(carry, piece, start):
        return attend(carry, piece, start)

    start_state = (
        jnp.full((KV_HEADS, group, rows), -1e30, jnp.float32),
        jnp.zeros((KV_HEADS, group, rows), jnp.float32),
        jnp.zeros((KV_HEADS, group, rows, HEAD_DIM), jnp.float32),
    )
    piece = lax.all_gather(kv_rows, "gy", axis=0, tiled=True)
    length = piece.shape[0]
    span = math.gcd(length, key_span)
    stacked = piece.reshape(length // span, span, piece.shape[1])
    offsets = jnp.arange(length // span, dtype=jnp.int32) * span

    def advance(state, item):
        return (visit(state, item[0], item[1]), None)

    final_state, unused = lax.scan(advance, start_state, (stacked, offsets))
    running, total, summed = final_state
    attn = (
        jnp.transpose(summed / total[..., None], (2, 0, 1, 3))
        .reshape(rows, qdim)
        .astype(jnp.bfloat16)
    )
    return (attn, kv_rows)


def solution(mesh):
    placed = (P(("gx", "gy"), None), P("gx", None), P(), P("gx", "gy"), P())
    return jax.shard_map(
        on_device,
        mesh=mesh,
        in_specs=placed,
        out_specs=(P(("gx", "gy"), None), P(("gx", "gy"), None)),
        check_vma=False,
    )
```

profile of v0, /device:TPU:0, one launch (start us, length us, event | category | flops | bytes accessed | tf_op | source)
XLA Modules:
  0.0 595.3 jit_solution(592481126304964280)
XLA Ops:
  7.2 0.7 all-gather.9.cloned.1.call-update
  7.9 1.9 fusion.17
  9.9 3.2 fusion.19
  13.2 0.8 dynamic_slice.11
  13.9 24.0 %all-gather.9.cloned.1.call-done = bf16[8,448,288]{1,2,0:T(8,128)(2,1)} async-done(((bf16[1,448,288]{1,2,0:T(8,128)(2,1)}), bf16[8,448,288]{1,2,0:T(8,128)(2,1)}) %all-gather.9.cloned.1.call-update) | async-done | bytes 2064400 | tf_op jit(solution)/shard_map/all_gather | solution.py:43
  38.0 3.0 copy.34
  41.0 3.6 reshape.172
  44.5 172.0 %all-gather.5.cloned.1.call-done = bf16[4096,3584]{1,0:T(8,128)(2,1)} async-done(((bf16[256,3584]{1,0:T(8,128)(2,1)}), bf16[4096,3584]{1,0:T(8,128)(2,1)}) %all-gather.5.cloned.1.call-update) | async-done | bytes 29360144 | tf_op jit(solution)/shard_map/all_gather | solution.py:40
  216.6 14.7 %fusion.16 = bf16[4096,288]{0,1:T(8,128)(2,1)S(1)} fusion(bf16[4096,3584]{1,0:T(8,128)(2,1)} %all-gather.5.cloned.1.call-done, bf16[3584,288]{0,1:T(8,128)(2,1)} %reshape.172, f32[288]{0:T(512)S(1)} %dynamic_slice.11), kind=kOutput, calls=%fused_computation.25 | convolution fusion | flops 8458076160 | bytes 33784960 | tf_op jit(solution)/shard_map/dot_general | solution.py:41
  231.3 1.7 copy.53
  233.0 5.3 all-to-all-start
  239.1 34.4 %all-to-all-done = bf16[16,256,288]{1,2,0:T(8,128)(2,1)S(1)} async-done(((bf16[16,256,288]{1,2,0:T(8,128)(2,1)}), bf16[16,256,288]{1,2,0:T(8,128)(2,1)S(1)}, u32[]{:S(2)}, u32[]{:S(2)}) %all-to-all-start) | async-done | bytes 2359328 | tf_op jit(solution)/shard_map/all_to_all | solution.py:49
  273.6 0.9 pad_maximum_fusion.1
  274.6 1.3 slice.42
  275.9 1.0 copy.40
  276.9 1.9 convert.19
  279.5 1.4 pad_maximum_fusion
  280.8 3.0 copy.37
  283.8 65.9 %all-gather.7.cloned.1.call-done = bf16[4096,1024]{0,1:T(8,128)(2,1)} async-done(((bf16[256,1024]{0,1:T(8,128)(2,1)}), bf16[4096,1024]{0,1:T(8,128)(2,1)}) %all-gather.7.cloned.1.call-update) | async-done | bytes 8388624 | tf_op jit(solution)/shard_map/all_gather | solution.py:106
  349.7 7.5 %copy.52 = bf16[128,8,8,512]{3,2,0,1:T(8,128)(2,1)} copy(bf16[128,8,8,512]{3,2,1,0:T(8,128)(2,1)} %bitcast.86) | data formatting | bytes 16777216 | tf_op jit(solution)/shard_map/reshape | solution.py:109
  357.2 222.0 %while.15 = (s32[]{:T(128)}, f32[4,7,256]{2,1,0:T(8,128)S(1)}, f32[4,7,256]{2,1,0:T(8,128)S(1)}, f32[4,7,256,128]{3,2,1,0:T(8,128)}, s32[256]{0:T(256)S(1)}, /*i...) while((s32[]{:T(128)}, f32[4,7,256]{2,1,0:T(8,128)S(1)}, ...), condition=%wide.region_8.9_spmd.clone, body=%wide.region_4.8_spmd.clone.sunk | while | flops 1922606336 | bytes 88814816 | solution.py:115
  358.7 1.3 dynamic-slice_bitcast_fusion.2
  360.1 6.5 %fusion.43 = (f32[4,7,256]{2,1,0:T(8,128)S(1)}, f32[4,512,256,7]{2,1,3,0:T(8,128)}) fusion(pred[256,512]{0,1:T(8,128)(4,1)S(1)} %compare_and_fusion.2, bf16[512,4,128,1]{0,2,3,1:T(8,128)(2,1)S(1)} %bitcast.80, bf16[256,4,7,128]{3,0,2,1:T(8,128)(2,1)S(1)} %get-tuple-element.270), kind=kOutput, calls=%fused_computation.3.clone.1 | convolution fusion | flops 950526976 | bytes 17199104 | tf_op jit(solution)/shard_map/while/body/eval_jaxpr/rgho,ngo->ghrn/dot_general | solution.py:80
  366.6 8.3 %fusion.44 = f32[4,7,256]{2,1,0:T(8,128)S(1)} fusion(f32[4,512,256,7]{2,1,3,0:T(8,128)} %get-tuple-element.234, f32[4,7,256]{2,1,0:T(8,128)S(1)} %select_maximum_fusion.2, pred[256,512]{0,1:T(8,128)(4,1)S(1)} %compare_and_fusion.2), kind=kLoop, calls=%fused_computation.7.clone.1 | loop fusion | flops 14672896 | bytes 14868480 | tf_op jit(solution)/shard_map/while/body/eval_jaxpr/reduce_sum | solution.py:89
  375.0 8.0 %fusion.46 = f32[4,7,256,128]{3,2,1,0:T(8,128)S(1)} fusion(f32[4,7,256,128]{3,2,1,0:T(8,128)S(1)} %copy-done.1, bf16[512,4,128,1]{0,2,3,1:T(8,128)(2,1)S(1)} %bitcast.82, f32[4,512,256,7]{2,1,3,0:T(8,128)} %get-tuple-element.234, f32[4,7,256]{2,1,0:T(8,128)S(1)} %select_maximum_fusion.2, pred[256,512]{0,1:T(8,128)(4,1)S(1)} %compare_and_fusion.2, ...), kind=kOutput, calls=%fused_computation.11.clone.1 | convolution fusion | flops 956956672 | bytes 22732800 | tf_op jit(solution)/shard_map/while/body/eval_jaxpr/ghrn,ngo->ghro/dot_general | solution.py:90
  383.0 1.9 copy-done.2
  386.5 1.3 dynamic-slice_bitcast_fusion.2
  387.8 6.5 %fusion.43 = (f32[4,7,256]{2,1,0:T(8,128)S(1)}, f32[4,512,256,7]{2,1,3,0:T(8,128)}) fusion(pred[256,512]{0,1:T(8,128)(4,1)S(1)} %compare_and_fusion.2, bf16[512,4,128,1]{0,2,3,1:T(8,128)(2,1)S(1)} %bitcast.80, bf16[256,4,7,128]{3,0,2,1:T(8,128)(2,1)S(1)} %get-tuple-element.270), kind=kOutput, calls=%fused_computation.3.clone.1 | convolution fusion | flops 950526976 | bytes 17199104 | tf_op jit(solution)/shard_map/while/body/eval_jaxpr/rgho,ngo->ghrn/dot_general | solution.py:80
  394.4 8.3 %fusion.44 = f32[4,7,256]{2,1,0:T(8,128)S(1)} fusion(f32[4,512,256,7]{2,1,3,0:T(8,128)} %get-tuple-element.234, f32[4,7,256]{2,1,0:T(8,128)S(1)} %select_maximum_fusion.2, pred[256,512]{0,1:T(8,128)(4,1)S(1)} %compare_and_fusion.2), kind=kLoop, calls=%fused_computation.7.clone.1 | loop fusion | flops 14672896 | bytes 14868480 | tf_op jit(solution)/shard_map/while/body/eval_jaxpr/reduce_sum | solution.py:89
  402.7 8.0 %fusion.46 = f32[4,7,256,128]{3,2,1,0:T(8,128)S(1)} fusion(f32[4,7,256,128]{3,2,1,0:T(8,128)S(1)} %copy-done.1, bf16[512,4,128,1]{0,2,3,1:T(8,128)(2,1)S(1)} %bitcast.82, f32[4,512,256,7]{2,1,3,0:T(8,128)} %get-tuple-element.234, f32[4,7,256]{2,1,0:T(8,128)S(1)} %select_maximum_fusion.2, pred[256,512]{0,1:T(8,128)(4,1)S(1)} %compare_and_fusion.2, ...), kind=kOutput, calls=%fused_computation.11.clone.1 | convolution fusion | flops 956956672 | bytes 22732800 | tf_op jit(solution)/shard_map/while/body/eval_jaxpr/ghrn,ngo->ghro/dot_general | solution.py:90
  410.8 1.9 copy-done.2
  414.2 1.3 dynamic-slice_bitcast_fusion.2
  415.6 6.5 %fusion.43 = (f32[4,7,256]{2,1,0:T(8,128)S(1)}, f32[4,512,256,7]{2,1,3,0:T(8,128)}) fusion(pred[256,512]{0,1:T(8,128)(4,1)S(1)} %compare_and_fusion.2, bf16[512,4,128,1]{0,2,3,1:T(8,128)(2,1)S(1)} %bitcast.80, bf16[256,4,7,128]{3,0,2,1:T(8,128)(2,1)S(1)} %get-tuple-element.270), kind=kOutput, calls=%fused_computation.3.clone.1 | convolution fusion | flops 950526976 | bytes 17199104 | tf_op jit(solution)/shard_map/while/body/eval_jaxpr/rgho,ngo->ghrn/dot_general | solution.py:80
  422.1 8.3 %fusion.44 = f32[4,7,256]{2,1,0:T(8,128)S(1)} fusion(f32[4,512,256,7]{2,1,3,0:T(8,128)} %get-tuple-element.234, f32[4,7,256]{2,1,0:T(8,128)S(1)} %select_maximum_fusion.2, pred[256,512]{0,1:T(8,128)(4,1)S(1)} %compare_and_fusion.2), kind=kLoop, calls=%fused_computation.7.clone.1 | loop fusion | flops 14672896 | bytes 14868480 | tf_op jit(solution)/shard_map/while/body/eval_jaxpr/reduce_sum | solution.py:89
  430.5 8.0 %fusion.46 = f32[4,7,256,128]{3,2,1,0:T(8,128)S(1)} fusion(f32[4,7,256,128]{3,2,1,0:T(8,128)S(1)} %copy-done.1, bf16[512,4,128,1]{0,2,3,1:T(8,128)(2,1)S(1)} %bitcast.82, f32[4,512,256,7]{2,1,3,0:T(8,128)} %get-tuple-element.234, f32[4,7,256]{2,1,0:T(8,128)S(1)} %select_maximum_fusion.2, pred[256,512]{0,1:T(8,128)(4,1)S(1)} %compare_and_fusion.2, ...), kind=kOutput, calls=%fused_computation.11.clone.1 | convolution fusion | flops 956956672 | bytes 22732800 | tf_op jit(solution)/shard_map/while/body/eval_jaxpr/ghrn,ngo->ghro/dot_general | solution.py:90
  438.5 1.9 copy-done.2
  441.9 1.3 dynamic-slice_bitcast_fusion.2
  443.3 6.5 %fusion.43 = (f32[4,7,256]{2,1,0:T(8,128)S(1)}, f32[4,512,256,7]{2,1,3,0:T(8,128)}) fusion(pred[256,512]{0,1:T(8,128)(4,1)S(1)} %compare_and_fusion.2, bf16[512,4,128,1]{0,2,3,1:T(8,128)(2,1)S(1)} %bitcast.80, bf16[256,4,7,128]{3,0,2,1:T(8,128)(2,1)S(1)} %get-tuple-element.270), kind=kOutput, calls=%fused_computation.3.clone.1 | convolution fusion | flops 950526976 | bytes 17199104 | tf_op jit(solution)/shard_map/while/body/eval_jaxpr/rgho,ngo->ghrn/dot_general | solution.py:80
  449.9 8.3 %fusion.44 = f32[4,7,256]{2,1,0:T(8,128)S(1)} fusion(f32[4,512,256,7]{2,1,3,0:T(8,128)} %get-tuple-element.234, f32[4,7,256]{2,1,0:T(8,128)S(1)} %select_maximum_fusion.2, pred[256,512]{0,1:T(8,128)(4,1)S(1)} %compare_and_fusion.2), kind=kLoop, calls=%fused_computation.7.clone.1 | loop fusion | flops 14672896 | bytes 14868480 | tf_op jit(solution)/shard_map/while/body/eval_jaxpr/reduce_sum | solution.py:89
  458.2 8.0 %fusion.46 = f32[4,7,256,128]{3,2,1,0:T(8,128)S(1)} fusion(f32[4,7,256,128]{3,2,1,0:T(8,128)S(1)} %copy-done.1, bf16[512,4,128,1]{0,2,3,1:T(8,128)(2,1)S(1)} %bitcast.82, f32[4,512,256,7]{2,1,3,0:T(8,128)} %get-tuple-element.234, f32[4,7,256]{2,1,0:T(8,128)S(1)} %select_maximum_fusion.2, pred[256,512]{0,1:T(8,128)(4,1)S(1)} %compare_and_fusion.2, ...), kind=kOutput, calls=%fused_computation.11.clone.1 | convolution fusion | flops 956956672 | bytes 22732800 | tf_op jit(solution)/shard_map/while/body/eval_jaxpr/ghrn,ngo->ghro/dot_general | solution.py:90
  466.3 1.9 copy-done.2
  469.7 1.3 dynamic-slice_bitcast_fusion.2
  471.1 6.5 %fusion.43 = (f32[4,7,256]{2,1,0:T(8,128)S(1)}, f32[4,512,256,7]{2,1,3,0:T(8,128)}) fusion(pred[256,512]{0,1:T(8,128)(4,1)S(1)} %compare_and_fusion.2, bf16[512,4,128,1]{0,2,3,1:T(8,128)(2,1)S(1)} %bitcast.80, bf16[256,4,7,128]{3,0,2,1:T(8,128)(2,1)S(1)} %get-tuple-element.270), kind=kOutput, calls=%fused_computation.3.clone.1 | convolution fusion | flops 950526976 | bytes 17199104 | tf_op jit(solution)/shard_map/while/body/eval_jaxpr/rgho,ngo->ghrn/dot_general | solution.py:80
  477.6 8.3 %fusion.44 = f32[4,7,256]{2,1,0:T(8,128)S(1)} fusion(f32[4,512,256,7]{2,1,3,0:T(8,128)} %get-tuple-element.234, f32[4,7,256]{2,1,0:T(8,128)S(1)} %select_maximum_fusion.2, pred[256,512]{0,1:T(8,128)(4,1)S(1)} %compare_and_fusion.2), kind=kLoop, calls=%fused_computation.7.clone.1 | loop fusion | flops 14672896 | bytes 14868480 | tf_op jit(solution)/shard_map/while/body/eval_jaxpr/reduce_sum | solution.py:89
  486.0 8.0 %fusion.46 = f32[4,7,256,128]{3,2,1,0:T(8,128)S(1)} fusion(f32[4,7,256,128]{3,2,1,0:T(8,128)S(1)} %copy-done.1, bf16[512,4,128,1]{0,2,3,1:T(8,128)(2,1)S(1)} %bitcast.82, f32[4,512,256,7]{2,1,3,0:T(8,128)} %get-tuple-element.234, f32[4,7,256]{2,1,0:T(8,128)S(1)} %select_maximum_fusion.2, pred[256,512]{0,1:T(8,128)(4,1)S(1)} %compare_and_fusion.2, ...), kind=kOutput, calls=%fused_computation.11.clone.1 | convolution fusion | flops 956956672 | bytes 22732800 | tf_op jit(solution)/shard_map/while/body/eval_jaxpr/ghrn,ngo->ghro/dot_general | solution.py:90
  494.0 1.9 copy-done.2
  497.4 1.3 dynamic-slice_bitcast_fusion.2
  498.8 6.5 %fusion.43 = (f32[4,7,256]{2,1,0:T(8,128)S(1)}, f32[4,512,256,7]{2,1,3,0:T(8,128)}) fusion(pred[256,512]{0,1:T(8,128)(4,1)S(1)} %compare_and_fusion.2, bf16[512,4,128,1]{0,2,3,1:T(8,128)(2,1)S(1)} %bitcast.80, bf16[256,4,7,128]{3,0,2,1:T(8,128)(2,1)S(1)} %get-tuple-element.270), kind=kOutput, calls=%fused_computation.3.clone.1 | convolution fusion | flops 950526976 | bytes 17199104 | tf_op jit(solution)/shard_map/while/body/eval_jaxpr/rgho,ngo->ghrn/dot_general | solution.py:80
  505.4 8.3 %fusion.44 = f32[4,7,256]{2,1,0:T(8,128)S(1)} fusion(f32[4,512,256,7]{2,1,3,0:T(8,128)} %get-tuple-element.234, f32[4,7,256]{2,1,0:T(8,128)S(1)} %select_maximum_fusion.2, pred[256,512]{0,1:T(8,128)(4,1)S(1)} %compare_and_fusion.2), kind=kLoop, calls=%fused_computation.7.clone.1 | loop fusion | flops 14672896 | bytes 14868480 | tf_op jit(solution)/shard_map/while/body/eval_jaxpr/reduce_sum | solution.py:89
  513.7 8.0 %fusion.46 = f32[4,7,256,128]{3,2,1,0:T(8,128)S(1)} fusion(f32[4,7,256,128]{3,2,1,0:T(8,128)S(1)} %copy-done.1, bf16[512,4,128,1]{0,2,3,1:T(8,128)(2,1)S(1)} %bitcast.82, f32[4,512,256,7]{2,1,3,0:T(8,128)} %get-tuple-element.234, f32[4,7,256]{2,1,0:T(8,128)S(1)} %select_maximum_fusion.2, pred[256,512]{0,1:T(8,128)(4,1)S(1)} %compare_and_fusion.2, ...), kind=kOutput, calls=%fused_computation.11.clone.1 | convolution fusion | flops 956956672 | bytes 22732800 | tf_op jit(solution)/shard_map/while/body/eval_jaxpr/ghrn,ngo->ghro/dot_general | solution.py:90
  521.8 1.9 copy-done.2
  525.2 1.3 dynamic-slice_bitcast_fusion.2
  526.6 6.5 %fusion.43 = (f32[4,7,256]{2,1,0:T(8,128)S(1)}, f32[4,512,256,7]{2,1,3,0:T(8,128)}) fusion(pred[256,512]{0,1:T(8,128)(4,1)S(1)} %compare_and_fusion.2, bf16[512,4,128,1]{0,2,3,1:T(8,128)(2,1)S(1)} %bitcast.80, bf16[256,4,7,128]{3,0,2,1:T(8,128)(2,1)S(1)} %get-tuple-element.270), kind=kOutput, calls=%fused_computation.3.clone.1 | convolution fusion | flops 950526976 | bytes 17199104 | tf_op jit(solution)/shard_map/while/body/eval_jaxpr/rgho,ngo->ghrn/dot_general | solution.py:80
  533.1 8.3 %fusion.44 = f32[4,7,256]{2,1,0:T(8,128)S(1)} fusion(f32[4,512,256,7]{2,1,3,0:T(8,128)} %get-tuple-element.234, f32[4,7,256]{2,1,0:T(8,128)S(1)} %select_maximum_fusion.2, pred[256,512]{0,1:T(8,128)(4,1)S(1)} %compare_and_fusion.2), kind=kLoop, calls=%fused_computation.7.clone.1 | loop fusion | flops 14672896 | bytes 14868480 | tf_op jit(solution)/shard_map/while/body/eval_jaxpr/reduce_sum | solution.py:89
  541.5 8.0 %fusion.46 = f32[4,7,256,128]{3,2,1,0:T(8,128)S(1)} fusion(f32[4,7,256,128]{3,2,1,0:T(8,128)S(1)} %copy-done.1, bf16[512,4,128,1]{0,2,3,1:T(8,128)(2,1)S(1)} %bitcast.82, f32[4,512,256,7]{2,1,3,0:T(8,128)} %get-tuple-element.234, f32[4,7,256]{2,1,0:T(8,128)S(1)} %select_maximum_fusion.2, pred[256,512]{0,1:T(8,128)(4,1)S(1)} %compare_and_fusion.2, ...), kind=kOutput, calls=%fused_computation.11.clone.1 | convolution fusion | flops 956956672 | bytes 22732800 | tf_op jit(solution)/shard_map/while/body/eval_jaxpr/ghrn,ngo->ghro/dot_general | solution.py:90
  549.5 1.9 copy-done.2
  552.9 1.3 dynamic-slice_bitcast_fusion.2
  554.3 6.5 %fusion.43 = (f32[4,7,256]{2,1,0:T(8,128)S(1)}, f32[4,512,256,7]{2,1,3,0:T(8,128)}) fusion(pred[256,512]{0,1:T(8,128)(4,1)S(1)} %compare_and_fusion.2, bf16[512,4,128,1]{0,2,3,1:T(8,128)(2,1)S(1)} %bitcast.80, bf16[256,4,7,128]{3,0,2,1:T(8,128)(2,1)S(1)} %get-tuple-element.270), kind=kOutput, calls=%fused_computation.3.clone.1 | convolution fusion | flops 950526976 | bytes 17199104 | tf_op jit(solution)/shard_map/while/body/eval_jaxpr/rgho,ngo->ghrn/dot_general | solution.py:80
  560.9 8.3 %fusion.44 = f32[4,7,256]{2,1,0:T(8,128)S(1)} fusion(f32[4,512,256,7]{2,1,3,0:T(8,128)} %get-tuple-element.234, f32[4,7,256]{2,1,0:T(8,128)S(1)} %select_maximum_fusion.2, pred[256,512]{0,1:T(8,128)(4,1)S(1)} %compare_and_fusion.2), kind=kLoop, calls=%fused_computation.7.clone.1 | loop fusion | flops 14672896 | bytes 14868480 | tf_op jit(solution)/shard_map/while/body/eval_jaxpr/reduce_sum | solution.py:89
  569.2 8.0 %fusion.46 = f32[4,7,256,128]{3,2,1,0:T(8,128)S(1)} fusion(f32[4,7,256,128]{3,2,1,0:T(8,128)S(1)} %copy-done.1, bf16[512,4,128,1]{0,2,3,1:T(8,128)(2,1)S(1)} %bitcast.82, f32[4,512,256,7]{2,1,3,0:T(8,128)} %get-tuple-element.234, f32[4,7,256]{2,1,0:T(8,128)S(1)} %select_maximum_fusion.2, pred[256,512]{0,1:T(8,128)(4,1)S(1)} %compare_and_fusion.2, ...), kind=kOutput, calls=%fused_computation.11.clone.1 | convolution fusion | flops 956956672 | bytes 22732800 | tf_op jit(solution)/shard_map/while/body/eval_jaxpr/ghrn,ngo->ghro/dot_general | solution.py:90
  577.3 1.9 copy-done.2
  579.1 4.6 copy.38
  583.7 2.5 divide_convert_fusion
  586.2 2.6 copy.39
  (121 shorter events, 14.8 us)
Async XLA Ops:
  7.2 30.8 %all-gather.9.cloned.1.call-start = ((), (), s32[]{:S(2)}) async-start(), calls=%async_computation.3 | async-start | bytes 2654208 | tf_op jit(solution)/shard_map/all_gather | solution.py:43
  7.9 208.7 %all-gather.5.cloned.1.call-start = ((), (), s32[]{:S(2)}) async-start(), calls=%async_computation.1 | async-start | bytes 31195136 | tf_op jit(solution)/shard_map/all_gather | solution.py:40
  231.3 7.2 %copy-start.3 = (s32[1,4]{1,0:T(1,128)S(1)}, s32[1,4]{1,0:T(1,128)}, u32[]{:S(2)}) copy-start(s32[1,4]{1,0:T(1,128)} %param.8) | copy-start | bytes 52
  233.0 40.5 %all-to-all-start = ((bf16[16,256,288]{1,2,0:T(8,128)(2,1)}), bf16[16,256,288]{1,2,0:T(8,128)(2,1)S(1)}, u32[]{:S(2)}, u32[]{:S(2)}) async-start(bf16[16,256,288]{1,2,0:T(8,128)(2,1)} %bitcast.85), calls=%async_computation | async-start | bytes 4718592 | tf_op jit(solution)/shard_map/all_to_all | solution.py:49
  238.2 111.5 %all-gather.7.cloned.1.call-start = ((), (), s32[]{:S(2)}) async-start(), calls=%async_computation.2 | async-start | bytes 8912896 | tf_op jit(solution)/shard_map/all_gather | solution.py:106
  274.5 1.4 copy-start
  366.6 8.4 %copy-start.1 = (f32[4,7,256,128]{3,2,1,0:T(8,128)S(1)}, f32[4,7,256,128]{3,2,1,0:T(8,128)}, u32[]{:S(2)}) copy-start(f32[4,7,256,128]{3,2,1,0:T(8,128)} %get-tuple-element.253) | copy-start | bytes 11010052 | tf_op jit(solution)/shard_map/while
  383.0 1.9 copy-start.2
  394.4 8.4 %copy-start.1 = (f32[4,7,256,128]{3,2,1,0:T(8,128)S(1)}, f32[4,7,256,128]{3,2,1,0:T(8,128)}, u32[]{:S(2)}) copy-start(f32[4,7,256,128]{3,2,1,0:T(8,128)} %get-tuple-element.253) | copy-start | bytes 11010052 | tf_op jit(solution)/shard_map/while
  410.8 1.9 copy-start.2
  422.1 8.4 %copy-start.1 = (f32[4,7,256,128]{3,2,1,0:T(8,128)S(1)}, f32[4,7,256,128]{3,2,1,0:T(8,128)}, u32[]{:S(2)}) copy-start(f32[4,7,256,128]{3,2,1,0:T(8,128)} %get-tuple-element.253) | copy-start | bytes 11010052 | tf_op jit(solution)/shard_map/while
  438.5 1.9 copy-start.2
  449.9 8.4 %copy-start.1 = (f32[4,7,256,128]{3,2,1,0:T(8,128)S(1)}, f32[4,7,256,128]{3,2,1,0:T(8,128)}, u32[]{:S(2)}) copy-start(f32[4,7,256,128]{3,2,1,0:T(8,128)} %get-tuple-element.253) | copy-start | bytes 11010052 | tf_op jit(solution)/shard_map/while
  466.3 1.9 copy-start.2
  477.6 8.4 %copy-start.1 = (f32[4,7,256,128]{3,2,1,0:T(8,128)S(1)}, f32[4,7,256,128]{3,2,1,0:T(8,128)}, u32[]{:S(2)}) copy-start(f32[4,7,256,128]{3,2,1,0:T(8,128)} %get-tuple-element.253) | copy-start | bytes 11010052 | tf_op jit(solution)/shard_map/while
  494.0 1.9 copy-start.2
  505.4 8.4 %copy-start.1 = (f32[4,7,256,128]{3,2,1,0:T(8,128)S(1)}, f32[4,7,256,128]{3,2,1,0:T(8,128)}, u32[]{:S(2)}) copy-start(f32[4,7,256,128]{3,2,1,0:T(8,128)} %get-tuple-element.253) | copy-start | bytes 11010052 | tf_op jit(solution)/shard_map/while
  521.8 1.9 copy-start.2
  533.1 8.4 %copy-start.1 = (f32[4,7,256,128]{3,2,1,0:T(8,128)S(1)}, f32[4,7,256,128]{3,2,1,0:T(8,128)}, u32[]{:S(2)}) copy-start(f32[4,7,256,128]{3,2,1,0:T(8,128)} %get-tuple-element.253) | copy-start | bytes 11010052 | tf_op jit(solution)/shard_map/while
  549.5 1.9 copy-start.2
  560.9 8.4 %copy-start.1 = (f32[4,7,256,128]{3,2,1,0:T(8,128)S(1)}, f32[4,7,256,128]{3,2,1,0:T(8,128)}, u32[]{:S(2)}) copy-start(f32[4,7,256,128]{3,2,1,0:T(8,128)} %get-tuple-element.253) | copy-start | bytes 11010052 | tf_op jit(solution)/shard_map/while
  577.3 1.9 copy-start.2
Sparse Core Ops, SparseCore 0:
  9.7 28.2 all-gather.8
  40.7 175.8 all-gather.4
  274.6 75.0 all-gather.6
where the time goes:
time: 597 us; the launch traced here: 595 us
  waiting for transfers between devices  297 us (50%)
  matrix products  131 us (22%)
  other arithmetic  87.5 us (15%)
  local copies, waits for them, and re-layouts  59.6 us (10%)
  between operations  13.9 us (2%)
    all_gather x1, waiting for transfers between devices, project_joined(): grouped = lax.all_gather(normed, 'gy', axis=0, tiled=True)  172 us
    reduce_sum x8, other arithmetic, attend(): total = total * shrink + jnp.sum(weights, axis=3)  66.5 us
    all_gather x1, waiting for transfers between devices, on_device(): piece = lax.all_gather(kv_rows, 'gy', axis=0, tiled=True)  65.9 us
    dot_general x8, matrix products, attend(): jnp.einsum('ghrn,ngo->ghro', weights.astype(jnp.bfloat16), value_part, pr...  64.3 us
    dot_general x8, matrix products, attend(): jnp.einsum('rgho,ngo->ghrn', queries, key_part, preferred_element_type=jn...  52.3 us
    all_to_all x1, waiting for transfers between devices, project_joined(): lax.all_to_all(block_out, 'gy', split_axis=0, concat_axis=1, tiled=True)  34.4 us
    all_gather x1, waiting for transfers between devices, project_joined(): lax.all_gather(weight, 'gx', axis=0, tiled=True)  24 us
    while x40, local copies, waits for them, and re-layouts  15 us
  transfers between devices with their start and end apart: 4, of which 4 were waited for; matrix products, arithmetic and copies ran while one was open for 4% of the time, Pallas kernels for 0%

commit v1 on v0

--- a/solution.py
+++ b/solution.py
@@ -8,6 +8,19 @@
 KV_HEADS = 4
 HEAD_DIM = 128
 key_span = 512
+
+
+def collect(shard, axis, dim):
+    ways = lax.axis_size(axis)
+    up = [(d, (d + 1) % ways) for d in range(ways)]
+    down = [(d, (d - 1) % ways) for d in range(ways)]
+    earlier, later = ([shard], [shard])
+    for _ in range(ways // 2):
+        earlier.append(lax.ppermute(earlier[-1], axis, up))
+    for _ in range((ways - 1) // 2):
+        later.append(lax.ppermute(later[-1], axis, down))
+    line = jnp.concatenate([*earlier[::-1], *later[1:]], axis=dim)
+    return jnp.roll(line, (lax.axis_index(axis) - ways // 2) * shard.shape[dim], axis=dim)
 
 
 def norm_rows(values, gain):
@@ -38,11 +51,7 @@
 
 def project_joined(normed, weight, bias):
     grouped = lax.all_gather(normed, "gy", axis=0, tiled=True)
-    summed = jnp.dot(
-        grouped,
-        lax.all_gather(weight, "gx", axis=0, tiled=True),
-        preferred_element_type=jnp.float32,
-    )
+    summed = jnp.dot(grouped, collect(weight, "gx", 0), preferred_element_type=jnp.float32)
     width = weight.shape[1]
     bias_block = lax.dynamic_slice_in_dim(bias, lax.axis_index("gy") * width, width, 0)
     block_out = (summed + bias_block[None, :]).astype(jnp.bfloat16)

time: 597 us -> 570 us (0.955)
  waiting for transfers between devices: 297 us -> 263 us
  starting transfers between devices: 5.55 us -> 15.1 us
    all_gather x1, waiting for transfers between devices: 172 us -> 143 us  [project_joined(): grouped = lax.all_gather(normed, 'gy', axis=0, tiled=True)]
    all_gather x1 -> x0, waiting for transfers between devices: 24 us -> none  [project_joined(): lax.all_gather(weight, 'gx', axis=0, tiled=True)]
    ppermute x0 -> x7, waiting for transfers between devices: none -> 19.7 us  [the longest x4 19.7 us: collect(): earlier.append(lax.ppermute(earlier[-1], axis, up))]
    ppermute x0 -> x7, starting transfers between devices: none -> 9.57 us  [the longest x3 9.54 us: collect(): later.append(lax.ppermute(later[-1], axis, down))]
  transfers between devices with their start and end apart: 4 -> 10, of which waited for: 4 -> 7; matrix products, arithmetic and copies ran while one was open for 4% -> 3% of each run, Pallas kernels for 0% -> 0%
where the time goes in v1:
time: 570 us; the launch traced here: 569 us
  waiting for transfers between devices  263 us (46%)
  matrix products  131 us (23%)
  other arithmetic  87.5 us (15%)
  local copies, waits for them, and re-layouts  58.1 us (10%)
  starting transfers between devices  15.1 us (3%)
  between operations  14.2 us (2%)
    all_gather x1, waiting for transfers between devices, project_joined(): grouped = lax.all_gather(normed, 'gy', axis=0, tiled=True)  143 us
    reduce_sum x8, other arithmetic, attend(): total = total * shrink + jnp.sum(weights, axis=3)  66.5 us
    all_gather x1, waiting for transfers between devices, on_device(): piece = lax.all_gather(kv_rows, 'gy', axis=0, tiled=True)  66 us
    dot_general x8, matrix products, attend(): jnp.einsum('ghrn,ngo->ghro', weights.astype(jnp.bfloat16), value_part, pr...  64.3 us
    dot_general x8, matrix products, attend(): jnp.einsum('rgho,ngo->ghrn', queries, key_part, preferred_element_type=jn...  51.8 us
    all_to_all x1, waiting for transfers between devices, project_joined(): lax.all_to_all(block_out, 'gy', split_axis=0, concat_axis=1, tiled=True)  34.4 us
    ppermute x4, waiting for transfers between devices, collect(): earlier.append(lax.ppermute(earlier[-1], axis, up))  19.7 us
    while x40, local copies, waits for them, and re-layouts  14.8 us
  transfers between devices with their start and end apart: 10, of which 7 were waited for; matrix products, arithmetic and copies ran while one was open for 3% of the time, Pallas kernels for 0%

profile of v1, /device:TPU:0, one launch (start us, length us, event | category | flops | bytes accessed | tf_op | source)
XLA Modules:
  0.0 569.1 jit_solution(3728094572263216327)
XLA Ops:
  7.2 2.0 fusion.17
  9.2 3.2 fusion.19
  12.5 3.6 collective-permute-start.4
  16.1 4.4 collective-permute-done
  20.5 3.0 collective-permute-start.5
  23.5 4.4 collective-permute-done.1
  27.9 3.0 collective-permute-start.6
  30.8 4.4 collective-permute-done.2
  36.0 6.6 %collective-permute-done.3 = bf16[448,288]{0,1:T(8,128)(2,1)S(1)} collective-permute-done((bf16[448,288]{0,1:T(8,128)(2,1)S(1)}, bf16[448,288]{0,1:T(8,128)(2,1)S(1)}, u32[]{:S(2)}, u32[]{:S(2)}) %collective-permute-start.3) | collective-permute-done | bytes 258080 | tf_op jit(solution)/shard_map/ppermute | solution.py:19
  42.6 5.2 concatenate.17
  47.7 142.8 %all-gather.3.cloned.1.call-done = bf16[4096,3584]{1,0:T(8,128)(2,1)} async-done(((bf16[256,3584]{1,0:T(8,128)(2,1)}), bf16[4096,3584]{1,0:T(8,128)(2,1)}) %all-gather.3.cloned.1.call-update) | async-done | bytes 29360144 | tf_op jit(solution)/shard_map/all_gather | solution.py:53
  190.5 14.8 %fusion.16 = bf16[4096,288]{0,1:T(8,128)(2,1)S(1)} fusion(bf16[4096,3584]{1,0:T(8,128)(2,1)} %all-gather.3.cloned.1.call-done, f32[288]{0:T(512)S(1)} %dynamic_slice.16, bf16[7168,288]{0,1:T(8,128)(2,1)} %concatenate.17, s32[]{:T(128)S(6)} %select_n.28), kind=kOutput, calls=%fused_computation.25 | convolution fusion | flops 8458076160 | bytes 33784964 | tf_op jit(solution)/shard_map/dot_general | solution.py:54
  205.3 1.7 copy.41
  207.0 5.3 all-to-all-start
  213.1 34.4 %all-to-all-done = bf16[16,256,288]{1,2,0:T(8,128)(2,1)S(1)} async-done(((bf16[16,256,288]{1,2,0:T(8,128)(2,1)}), bf16[16,256,288]{1,2,0:T(8,128)(2,1)S(1)}, u32[]{:S(2)}, u32[]{:S(2)}) %all-to-all-start) | async-done | bytes 2359328 | tf_op jit(solution)/shard_map/all_to_all | solution.py:58
  248.6 1.3 slice.42
  250.9 1.9 convert.19
  253.5 1.4 pad_maximum_fusion
  254.9 3.0 copy.25
  257.8 66.0 %all-gather.5.cloned.1.call-done = bf16[4096,1024]{0,1:T(8,128)(2,1)} async-done(((bf16[256,1024]{0,1:T(8,128)(2,1)}), bf16[4096,1024]{0,1:T(8,128)(2,1)}) %all-gather.5.cloned.1.call-update) | async-done | bytes 8388624 | tf_op jit(solution)/shard_map/all_gather | solution.py:115
  323.8 7.5 %copy.40 = bf16[128,8,8,512]{3,2,0,1:T(8,128)(2,1)} copy(bf16[128,8,8,512]{3,2,1,0:T(8,128)(2,1)} %bitcast.82) | data formatting | bytes 16777216 | tf_op jit(solution)/shard_map/reshape | solution.py:118
  331.3 221.3 %while.15 = (s32[]{:T(128)}, f32[4,7,256]{2,1,0:T(8,128)S(1)}, f32[4,7,256]{2,1,0:T(8,128)S(1)}, f32[4,7,256,128]{3,2,1,0:T(8,128)}, s32[256]{0:T(256)S(1)}, /*i...) while((s32[]{:T(128)}, f32[4,7,256]{2,1,0:T(8,128)S(1)}, ...), condition=%wide.region_8.9_spmd.clone, body=%wide.region_4.8_spmd.clone.sunk | while | flops 1922606336 | bytes 88814816 | solution.py:124
  332.8 1.3 dynamic-slice_bitcast_fusion.2
  334.2 6.5 %fusion.44 = (f32[4,7,256]{2,1,0:T(8,128)S(1)}, f32[4,512,256,7]{2,1,3,0:T(8,128)}) fusion(pred[256,512]{0,1:T(8,128)(4,1)S(1)} %compare_and_fusion.2, bf16[512,4,128,1]{0,2,3,1:T(8,128)(2,1)S(1)} %bitcast.76, bf16[256,4,7,128]{3,0,2,1:T(8,128)(2,1)S(1)} %get-tuple-element.258), kind=kOutput, calls=%fused_computation.3.clone.1 | convolution fusion | flops 950526976 | bytes 17199104 | tf_op jit(solution)/shard_map/while/body/eval_jaxpr/rgho,ngo->ghrn/dot_general | solution.py:89
  340.7 8.3 %fusion.45 = f32[4,7,256]{2,1,0:T(8,128)S(1)} fusion(f32[4,512,256,7]{2,1,3,0:T(8,128)} %get-tuple-element.222, f32[4,7,256]{2,1,0:T(8,128)S(1)} %select_maximum_fusion.2, pred[256,512]{0,1:T(8,128)(4,1)S(1)} %compare_and_fusion.2), kind=kLoop, calls=%fused_computation.7.clone.1 | loop fusion | flops 14672896 | bytes 14868480 | tf_op jit(solution)/shard_map/while/body/eval_jaxpr/reduce_sum | solution.py:98
  349.1 8.0 %fusion.47 = f32[4,7,256,128]{3,2,1,0:T(8,128)S(1)} fusion(f32[4,7,256,128]{3,2,1,0:T(8,128)S(1)} %copy-done.1, bf16[512,4,128,1]{0,2,3,1:T(8,128)(2,1)S(1)} %bitcast.78, f32[4,512,256,7]{2,1,3,0:T(8,128)} %get-tuple-element.222, f32[4,7,256]{2,1,0:T(8,128)S(1)} %select_maximum_fusion.2, pred[256,512]{0,1:T(8,128)(4,1)S(1)} %compare_and_fusion.2, ...), kind=kOutput, calls=%fused_computation.11.clone.1 | convolution fusion | flops 956956672 | bytes 22732800 | tf_op jit(solution)/shard_map/while/body/eval_jaxpr/ghrn,ngo->ghro/dot_general | solution.py:99
  357.1 1.8 copy-done.2
  360.5 1.3 dynamic-slice_bitcast_fusion.2
  361.9 6.5 %fusion.44 = (f32[4,7,256]{2,1,0:T(8,128)S(1)}, f32[4,512,256,7]{2,1,3,0:T(8,128)}) fusion(pred[256,512]{0,1:T(8,128)(4,1)S(1)} %compare_and_fusion.2, bf16[512,4,128,1]{0,2,3,1:T(8,128)(2,1)S(1)} %bitcast.76, bf16[256,4,7,128]{3,0,2,1:T(8,128)(2,1)S(1)} %get-tuple-element.258), kind=kOutput, calls=%fused_computation.3.clone.1 | convolution fusion | flops 950526976 | bytes 17199104 | tf_op jit(solution)/shard_map/while/body/eval_jaxpr/rgho,ngo->ghrn/dot_general | solution.py:89
  368.4 8.3 %fusion.45 = f32[4,7,256]{2,1,0:T(8,128)S(1)} fusion(f32[4,512,256,7]{2,1,3,0:T(8,128)} %get-tuple-element.222, f32[4,7,256]{2,1,0:T(8,128)S(1)} %select_maximum_fusion.2, pred[256,512]{0,1:T(8,128)(4,1)S(1)} %compare_and_fusion.2), kind=kLoop, calls=%fused_computation.7.clone.1 | loop fusion | flops 14672896 | bytes 14868480 | tf_op jit(solution)/shard_map/while/body/eval_jaxpr/reduce_sum | solution.py:98
  376.7 8.0 %fusion.47 = f32[4,7,256,128]{3,2,1,0:T(8,128)S(1)} fusion(f32[4,7,256,128]{3,2,1,0:T(8,128)S(1)} %copy-done.1, bf16[512,4,128,1]{0,2,3,1:T(8,128)(2,1)S(1)} %bitcast.78, f32[4,512,256,7]{2,1,3,0:T(8,128)} %get-tuple-element.222, f32[4,7,256]{2,1,0:T(8,128)S(1)} %select_maximum_fusion.2, pred[256,512]{0,1:T(8,128)(4,1)S(1)} %compare_and_fusion.2, ...), kind=kOutput, calls=%fused_computation.11.clone.1 | convolution fusion | flops 956956672 | bytes 22732800 | tf_op jit(solution)/shard_map/while/body/eval_jaxpr/ghrn,ngo->ghro/dot_general | solution.py:99
  384.8 1.8 copy-done.2
  388.2 1.3 dynamic-slice_bitcast_fusion.2
  389.5 6.5 %fusion.44 = (f32[4,7,256]{2,1,0:T(8,128)S(1)}, f32[4,512,256,7]{2,1,3,0:T(8,128)}) fusion(pred[256,512]{0,1:T(8,128)(4,1)S(1)} %compare_and_fusion.2, bf16[512,4,128,1]{0,2,3,1:T(8,128)(2,1)S(1)} %bitcast.76, bf16[256,4,7,128]{3,0,2,1:T(8,128)(2,1)S(1)} %get-tuple-element.258), kind=kOutput, calls=%fused_computation.3.clone.1 | convolution fusion | flops 950526976 | bytes 17199104 | tf_op jit(solution)/shard_map/while/body/eval_jaxpr/rgho,ngo->ghrn/dot_general | solution.py:89
  396.0 8.3 %fusion.45 = f32[4,7,256]{2,1,0:T(8,128)S(1)} fusion(f32[4,512,256,7]{2,1,3,0:T(8,128)} %get-tuple-element.222, f32[4,7,256]{2,1,0:T(8,128)S(1)} %select_maximum_fusion.2, pred[256,512]{0,1:T(8,128)(4,1)S(1)} %compare_and_fusion.2), kind=kLoop, calls=%fused_computation.7.clone.1 | loop fusion | flops 14672896 | bytes 14868480 | tf_op jit(solution)/shard_map/while/body/eval_jaxpr/reduce_sum | solution.py:98
  404.4 8.0 %fusion.47 = f32[4,7,256,128]{3,2,1,0:T(8,128)S(1)} fusion(f32[4,7,256,128]{3,2,1,0:T(8,128)S(1)} %copy-done.1, bf16[512,4,128,1]{0,2,3,1:T(8,128)(2,1)S(1)} %bitcast.78, f32[4,512,256,7]{2,1,3,0:T(8,128)} %get-tuple-element.222, f32[4,7,256]{2,1,0:T(8,128)S(1)} %select_maximum_fusion.2, pred[256,512]{0,1:T(8,128)(4,1)S(1)} %compare_and_fusion.2, ...), kind=kOutput, calls=%fused_computation.11.clone.1 | convolution fusion | flops 956956672 | bytes 22732800 | tf_op jit(solution)/shard_map/while/body/eval_jaxpr/ghrn,ngo->ghro/dot_general | solution.py:99
  412.4 1.8 copy-done.2
  417.2 6.5 %fusion.44 = (f32[4,7,256]{2,1,0:T(8,128)S(1)}, f32[4,512,256,7]{2,1,3,0:T(8,128)}) fusion(pred[256,512]{0,1:T(8,128)(4,1)S(1)} %compare_and_fusion.2, bf16[512,4,128,1]{0,2,3,1:T(8,128)(2,1)S(1)} %bitcast.76, bf16[256,4,7,128]{3,0,2,1:T(8,128)(2,1)S(1)} %get-tuple-element.258), kind=kOutput, calls=%fused_computation.3.clone.1 | convolution fusion | flops 950526976 | bytes 17199104 | tf_op jit(solution)/shard_map/while/body/eval_jaxpr/rgho,ngo->ghrn/dot_general | solution.py:89
  423.7 8.3 %fusion.45 = f32[4,7,256]{2,1,0:T(8,128)S(1)} fusion(f32[4,512,256,7]{2,1,3,0:T(8,128)} %get-tuple-element.222, f32[4,7,256]{2,1,0:T(8,128)S(1)} %select_maximum_fusion.2, pred[256,512]{0,1:T(8,128)(4,1)S(1)} %compare_and_fusion.2), kind=kLoop, calls=%fused_computation.7.clone.1 | loop fusion | flops 14672896 | bytes 14868480 | tf_op jit(solution)/shard_map/while/body/eval_jaxpr/reduce_sum | solution.py:98
  432.1 8.0 %fusion.47 = f32[4,7,256,128]{3,2,1,0:T(8,128)S(1)} fusion(f32[4,7,256,128]{3,2,1,0:T(8,128)S(1)} %copy-done.1, bf16[512,4,128,1]{0,2,3,1:T(8,128)(2,1)S(1)} %bitcast.78, f32[4,512,256,7]{2,1,3,0:T(8,128)} %get-tuple-element.222, f32[4,7,256]{2,1,0:T(8,128)S(1)} %select_maximum_fusion.2, pred[256,512]{0,1:T(8,128)(4,1)S(1)} %compare_and_fusion.2, ...), kind=kOutput, calls=%fused_computation.11.clone.1 | convolution fusion | flops 956956672 | bytes 22732800 | tf_op jit(solution)/shard_map/while/body/eval_jaxpr/ghrn,ngo->ghro/dot_general | solution.py:99
  440.1 1.8 copy-done.2
  443.5 1.3 dynamic-slice_bitcast_fusion.2
  444.9 6.5 %fusion.44 = (f32[4,7,256]{2,1,0:T(8,128)S(1)}, f32[4,512,256,7]{2,1,3,0:T(8,128)}) fusion(pred[256,512]{0,1:T(8,128)(4,1)S(1)} %compare_and_fusion.2, bf16[512,4,128,1]{0,2,3,1:T(8,128)(2,1)S(1)} %bitcast.76, bf16[256,4,7,128]{3,0,2,1:T(8,128)(2,1)S(1)} %get-tuple-element.258), kind=kOutput, calls=%fused_computation.3.clone.1 | convolution fusion | flops 950526976 | bytes 17199104 | tf_op jit(solution)/shard_map/while/body/eval_jaxpr/rgho,ngo->ghrn/dot_general | solution.py:89
  451.4 8.3 %fusion.45 = f32[4,7,256]{2,1,0:T(8,128)S(1)} fusion(f32[4,512,256,7]{2,1,3,0:T(8,128)} %get-tuple-element.222, f32[4,7,256]{2,1,0:T(8,128)S(1)} %select_maximum_fusion.2, pred[256,512]{0,1:T(8,128)(4,1)S(1)} %compare_and_fusion.2), kind=kLoop, calls=%fused_computation.7.clone.1 | loop fusion | flops 14672896 | bytes 14868480 | tf_op jit(solution)/shard_map/while/body/eval_jaxpr/reduce_sum | solution.py:98
  459.7 8.0 %fusion.47 = f32[4,7,256,128]{3,2,1,0:T(8,128)S(1)} fusion(f32[4,7,256,128]{3,2,1,0:T(8,128)S(1)} %copy-done.1, bf16[512,4,128,1]{0,2,3,1:T(8,128)(2,1)S(1)} %bitcast.78, f32[4,512,256,7]{2,1,3,0:T(8,128)} %get-tuple-element.222, f32[4,7,256]{2,1,0:T(8,128)S(1)} %select_maximum_fusion.2, pred[256,512]{0,1:T(8,128)(4,1)S(1)} %compare_and_fusion.2, ...), kind=kOutput, calls=%fused_computation.11.clone.1 | convolution fusion | flops 956956672 | bytes 22732800 | tf_op jit(solution)/shard_map/while/body/eval_jaxpr/ghrn,ngo->ghro/dot_general | solution.py:99
  467.8 1.8 copy-done.2
  471.2 1.3 dynamic-slice_bitcast_fusion.2
  472.5 6.5 %fusion.44 = (f32[4,7,256]{2,1,0:T(8,128)S(1)}, f32[4,512,256,7]{2,1,3,0:T(8,128)}) fusion(pred[256,512]{0,1:T(8,128)(4,1)S(1)} %compare_and_fusion.2, bf16[512,4,128,1]{0,2,3,1:T(8,128)(2,1)S(1)} %bitcast.76, bf16[256,4,7,128]{3,0,2,1:T(8,128)(2,1)S(1)} %get-tuple-element.258), kind=kOutput, calls=%fused_computation.3.clone.1 | convolution fusion | flops 950526976 | bytes 17199104 | tf_op jit(solution)/shard_map/while/body/eval_jaxpr/rgho,ngo->ghrn/dot_general | solution.py:89
  479.0 8.3 %fusion.45 = f32[4,7,256]{2,1,0:T(8,128)S(1)} fusion(f32[4,512,256,7]{2,1,3,0:T(8,128)} %get-tuple-element.222, f32[4,7,256]{2,1,0:T(8,128)S(1)} %select_maximum_fusion.2, pred[256,512]{0,1:T(8,128)(4,1)S(1)} %compare_and_fusion.2), kind=kLoop, calls=%fused_computation.7.clone.1 | loop fusion | flops 14672896 | bytes 14868480 | tf_op jit(solution)/shard_map/while/body/eval_jaxpr/reduce_sum | solution.py:98
  487.4 8.0 %fusion.47 = f32[4,7,256,128]{3,2,1,0:T(8,128)S(1)} fusion(f32[4,7,256,128]{3,2,1,0:T(8,128)S(1)} %copy-done.1, bf16[512,4,128,1]{0,2,3,1:T(8,128)(2,1)S(1)} %bitcast.78, f32[4,512,256,7]{2,1,3,0:T(8,128)} %get-tuple-element.222, f32[4,7,256]{2,1,0:T(8,128)S(1)} %select_maximum_fusion.2, pred[256,512]{0,1:T(8,128)(4,1)S(1)} %compare_and_fusion.2, ...), kind=kOutput, calls=%fused_computation.11.clone.1 | convolution fusion | flops 956956672 | bytes 22732800 | tf_op jit(solution)/shard_map/while/body/eval_jaxpr/ghrn,ngo->ghro/dot_general | solution.py:99
  495.4 1.8 copy-done.2
  498.8 1.3 dynamic-slice_bitcast_fusion.2
  500.2 6.5 %fusion.44 = (f32[4,7,256]{2,1,0:T(8,128)S(1)}, f32[4,512,256,7]{2,1,3,0:T(8,128)}) fusion(pred[256,512]{0,1:T(8,128)(4,1)S(1)} %compare_and_fusion.2, bf16[512,4,128,1]{0,2,3,1:T(8,128)(2,1)S(1)} %bitcast.76, bf16[256,4,7,128]{3,0,2,1:T(8,128)(2,1)S(1)} %get-tuple-element.258), kind=kOutput, calls=%fused_computation.3.clone.1 | convolution fusion | flops 950526976 | bytes 17199104 | tf_op jit(solution)/shard_map/while/body/eval_jaxpr/rgho,ngo->ghrn/dot_general | solution.py:89
  506.7 8.3 %fusion.45 = f32[4,7,256]{2,1,0:T(8,128)S(1)} fusion(f32[4,512,256,7]{2,1,3,0:T(8,128)} %get-tuple-element.222, f32[4,7,256]{2,1,0:T(8,128)S(1)} %select_maximum_fusion.2, pred[256,512]{0,1:T(8,128)(4,1)S(1)} %compare_and_fusion.2), kind=kLoop, calls=%fused_computation.7.clone.1 | loop fusion | flops 14672896 | bytes 14868480 | tf_op jit(solution)/shard_map/while/body/eval_jaxpr/reduce_sum | solution.py:98
  515.0 8.0 %fusion.47 = f32[4,7,256,128]{3,2,1,0:T(8,128)S(1)} fusion(f32[4,7,256,128]{3,2,1,0:T(8,128)S(1)} %copy-done.1, bf16[512,4,128,1]{0,2,3,1:T(8,128)(2,1)S(1)} %bitcast.78, f32[4,512,256,7]{2,1,3,0:T(8,128)} %get-tuple-element.222, f32[4,7,256]{2,1,0:T(8,128)S(1)} %select_maximum_fusion.2, pred[256,512]{0,1:T(8,128)(4,1)S(1)} %compare_and_fusion.2, ...), kind=kOutput, calls=%fused_computation.11.clone.1 | convolution fusion | flops 956956672 | bytes 22732800 | tf_op jit(solution)/shard_map/while/body/eval_jaxpr/ghrn,ngo->ghro/dot_general | solution.py:99
  523.1 1.8 copy-done.2
  526.5 1.3 dynamic-slice_bitcast_fusion.2
  527.9 6.5 %fusion.44 = (f32[4,7,256]{2,1,0:T(8,128)S(1)}, f32[4,512,256,7]{2,1,3,0:T(8,128)}) fusion(pred[256,512]{0,1:T(8,128)(4,1)S(1)} %compare_and_fusion.2, bf16[512,4,128,1]{0,2,3,1:T(8,128)(2,1)S(1)} %bitcast.76, bf16[256,4,7,128]{3,0,2,1:T(8,128)(2,1)S(1)} %get-tuple-element.258), kind=kOutput, calls=%fused_computation.3.clone.1 | convolution fusion | flops 950526976 | bytes 17199104 | tf_op jit(solution)/shard_map/while/body/eval_jaxpr/rgho,ngo->ghrn/dot_general | solution.py:89
  534.4 8.3 %fusion.45 = f32[4,7,256]{2,1,0:T(8,128)S(1)} fusion(f32[4,512,256,7]{2,1,3,0:T(8,128)} %get-tuple-element.222, f32[4,7,256]{2,1,0:T(8,128)S(1)} %select_maximum_fusion.2, pred[256,512]{0,1:T(8,128)(4,1)S(1)} %compare_and_fusion.2), kind=kLoop, calls=%fused_computation.7.clone.1 | loop fusion | flops 14672896 | bytes 14868480 | tf_op jit(solution)/shard_map/while/body/eval_jaxpr/reduce_sum | solution.py:98
  542.7 8.0 %fusion.47 = f32[4,7,256,128]{3,2,1,0:T(8,128)S(1)} fusion(f32[4,7,256,128]{3,2,1,0:T(8,128)S(1)} %copy-done.1, bf16[512,4,128,1]{0,2,3,1:T(8,128)(2,1)S(1)} %bitcast.78, f32[4,512,256,7]{2,1,3,0:T(8,128)} %get-tuple-element.222, f32[4,7,256]{2,1,0:T(8,128)S(1)} %select_maximum_fusion.2, pred[256,512]{0,1:T(8,128)(4,1)S(1)} %compare_and_fusion.2, ...), kind=kOutput, calls=%fused_computation.11.clone.1 | convolution fusion | flops 956956672 | bytes 22732800 | tf_op jit(solution)/shard_map/while/body/eval_jaxpr/ghrn,ngo->ghro/dot_general | solution.py:99
  550.8 1.8 copy-done.2
  552.6 4.7 copy.26
  557.3 2.5 divide_convert_fusion
  559.7 2.6 copy.27
  (133 shorter events, 18.8 us)
Async XLA Ops:
  7.2 5.3 copy-start.3
  7.2 183.3 %all-gather.3.cloned.1.call-start = ((), (), s32[]{:S(2)}) async-start(), calls=%async_computation.1 | async-start | bytes 31195136 | tf_op jit(solution)/shard_map/all_gather | solution.py:53
  12.5 8.0 %collective-permute-start = (bf16[448,288]{0,1:T(8,128)(2,1)S(1)}, bf16[448,288]{0,1:T(8,128)(2,1)S(1)}, u32[]{:S(2)}, u32[]{:S(2)}) collective-permute-start(bf16[448,288]{0,1:T(8,128)(2,1)S(1)} %copy-done.3), channel_id=1, source_target_pairs={{0,16},{16,32},{32,48},{48,64},{64,80},{80,96},{96,112},{112,0},{1... | collective-permute-start | bytes 774152 | tf_op jit(solution)/shard_map/ppermute | solution.py:19
  12.5 8.0 %collective-permute-start.4 = (bf16[448,288]{0,1:T(8,128)(2,1)S(1)}, bf16[448,288]{0,1:T(8,128)(2,1)S(1)}, u32[]{:S(2)}, u32[]{:S(2)}) collective-permute-start(bf16[448,288]{0,1:T(8,128)(2,1)S(1)} %copy-done.3), channel_id=1, source_target_pairs={{0,112},{16,0},{32,16},{48,32},{64,48},{80,64},{96,80},{112,96},{1... | collective-permute-start | bytes 774152 | tf_op jit(solution)/shard_map/ppermute | solution.py:21
  20.5 7.4 %collective-permute-start.1 = (bf16[448,288]{0,1:T(8,128)(2,1)S(1)}, bf16[448,288]{0,1:T(8,128)(2,1)S(1)}, u32[]{:S(2)}, u32[]{:S(2)}) collective-permute-start(bf16[448,288]{0,1:T(8,128)(2,1)S(1)} %collective-permute-done), channel_id=1, source_target_pairs={{0,16},{16,32},{32,48},{48,64},{64,80},{80,96},{96,112},{112,0},{1... | collective-permute-start | bytes 774152 | tf_op jit(solution)/shard_map/ppermute | solution.py:19
  20.5 7.4 %collective-permute-start.5 = (bf16[448,288]{0,1:T(8,128)(2,1)S(1)}, bf16[448,288]{0,1:T(8,128)(2,1)S(1)}, u32[]{:S(2)}, u32[]{:S(2)}) collective-permute-start(bf16[448,288]{0,1:T(8,128)(2,1)S(1)} %collective-permute-done.4), channel_id=1, source_target_pairs={{0,112},{16,0},{32,16},{48,32},{64,48},{80,64},{96,80},{112,96},{1... | collective-permute-start | bytes 774152 | tf_op jit(solution)/shard_map/ppermute | solution.py:21
  27.9 7.4 %collective-permute-start.2 = (bf16[448,288]{0,1:T(8,128)(2,1)S(1)}, bf16[448,288]{0,1:T(8,128)(2,1)S(1)}, u32[]{:S(2)}, u32[]{:S(2)}) collective-permute-start(bf16[448,288]{0,1:T(8,128)(2,1)S(1)} %collective-permute-done.1), channel_id=1, source_target_pairs={{0,16},{16,32},{32,48},{48,64},{64,80},{80,96},{96,112},{112,0},{1... | collective-permute-start | bytes 774152 | tf_op jit(solution)/shard_map/ppermute | solution.py:19
  27.9 8.1 %collective-permute-start.6 = (bf16[448,288]{0,1:T(8,128)(2,1)S(1)}, bf16[448,288]{0,1:T(8,128)(2,1)S(1)}, u32[]{:S(2)}, u32[]{:S(2)}) collective-permute-start(bf16[448,288]{0,1:T(8,128)(2,1)S(1)} %collective-permute-done.5), channel_id=1, source_target_pairs={{0,112},{16,0},{32,16},{48,32},{64,48},{80,64},{96,80},{112,96},{1... | collective-permute-start | bytes 774152 | tf_op jit(solution)/shard_map/ppermute | solution.py:21
  35.2 7.4 %collective-permute-start.3 = (bf16[448,288]{0,1:T(8,128)(2,1)S(1)}, bf16[448,288]{0,1:T(8,128)(2,1)S(1)}, u32[]{:S(2)}, u32[]{:S(2)}) collective-permute-start(bf16[448,288]{0,1:T(8,128)(2,1)S(1)} %collective-permute-done.2), channel_id=1, source_target_pairs={{0,16},{16,32},{32,48},{48,64},{64,80},{80,96},{96,112},{112,0},{1... | collective-permute-start | bytes 774152 | tf_op jit(solution)/shard_map/ppermute | solution.py:19
  205.3 7.2 %copy-start.4 = (s32[1,4]{1,0:T(1,128)S(1)}, s32[1,4]{1,0:T(1,128)}, u32[]{:S(2)}) copy-start(s32[1,4]{1,0:T(1,128)} %param.8) | copy-start | bytes 52
  207.0 40.5 %all-to-all-start = ((bf16[16,256,288]{1,2,0:T(8,128)(2,1)}), bf16[16,256,288]{1,2,0:T(8,128)(2,1)S(1)}, u32[]{:S(2)}, u32[]{:S(2)}) async-start(bf16[16,256,288]{1,2,0:T(8,128)(2,1)} %bitcast.81), calls=%async_computation | async-start | bytes 4718592 | tf_op jit(solution)/shard_map/all_to_all | solution.py:58
  212.2 111.6 %all-gather.5.cloned.1.call-start = ((), (), s32[]{:S(2)}) async-start(), calls=%async_computation.2 | async-start | bytes 8912896 | tf_op jit(solution)/shard_map/all_gather | solution.py:115
  248.5 1.4 copy-start
  340.7 8.4 %copy-start.1 = (f32[4,7,256,128]{3,2,1,0:T(8,128)S(1)}, f32[4,7,256,128]{3,2,1,0:T(8,128)}, u32[]{:S(2)}) copy-start(f32[4,7,256,128]{3,2,1,0:T(8,128)} %get-tuple-element.241) | copy-start | bytes 11010052 | tf_op jit(solution)/shard_map/while
  357.1 1.9 copy-start.2
  368.4 8.4 %copy-start.1 = (f32[4,7,256,128]{3,2,1,0:T(8,128)S(1)}, f32[4,7,256,128]{3,2,1,0:T(8,128)}, u32[]{:S(2)}) copy-start(f32[4,7,256,128]{3,2,1,0:T(8,128)} %get-tuple-element.241) | copy-start | bytes 11010052 | tf_op jit(solution)/shard_map/while
  384.8 1.9 copy-start.2
  396.0 8.4 %copy-start.1 = (f32[4,7,256,128]{3,2,1,0:T(8,128)S(1)}, f32[4,7,256,128]{3,2,1,0:T(8,128)}, u32[]{:S(2)}) copy-start(f32[4,7,256,128]{3,2,1,0:T(8,128)} %get-tuple-element.241) | copy-start | bytes 11010052 | tf_op jit(solution)/shard_map/while
  412.4 1.9 copy-start.2
  423.7 8.4 %copy-start.1 = (f32[4,7,256,128]{3,2,1,0:T(8,128)S(1)}, f32[4,7,256,128]{3,2,1,0:T(8,128)}, u32[]{:S(2)}) copy-start(f32[4,7,256,128]{3,2,1,0:T(8,128)} %get-tuple-element.241) | copy-start | bytes 11010052 | tf_op jit(solution)/shard_map/while
  440.1 1.9 copy-start.2
  451.4 8.4 %copy-start.1 = (f32[4,7,256,128]{3,2,1,0:T(8,128)S(1)}, f32[4,7,256,128]{3,2,1,0:T(8,128)}, u32[]{:S(2)}) copy-start(f32[4,7,256,128]{3,2,1,0:T(8,128)} %get-tuple-element.241) | copy-start | bytes 11010052 | tf_op jit(solution)/shard_map/while
  467.8 1.9 copy-start.2
  479.0 8.4 %copy-start.1 = (f32[4,7,256,128]{3,2,1,0:T(8,128)S(1)}, f32[4,7,256,128]{3,2,1,0:T(8,128)}, u32[]{:S(2)}) copy-start(f32[4,7,256,128]{3,2,1,0:T(8,128)} %get-tuple-element.241) | copy-start | bytes 11010052 | tf_op jit(solution)/shard_map/while
  495.4 1.9 copy-start.2
  506.7 8.4 %copy-start.1 = (f32[4,7,256,128]{3,2,1,0:T(8,128)S(1)}, f32[4,7,256,128]{3,2,1,0:T(8,128)}, u32[]{:S(2)}) copy-start(f32[4,7,256,128]{3,2,1,0:T(8,128)} %get-tuple-element.241) | copy-start | bytes 11010052 | tf_op jit(solution)/shard_map/while
  523.1 1.9 copy-start.2
  534.4 8.4 %copy-start.1 = (f32[4,7,256,128]{3,2,1,0:T(8,128)S(1)}, f32[4,7,256,128]{3,2,1,0:T(8,128)}, u32[]{:S(2)}) copy-start(f32[4,7,256,128]{3,2,1,0:T(8,128)} %get-tuple-element.241) | copy-start | bytes 11010052 | tf_op jit(solution)/shard_map/while
  550.8 1.9 copy-start.2
Sparse Core Ops, SparseCore 0:
  12.6 177.8 all-gather.2
  248.7 75.1 all-gather.4
